TPU v7x, 256 devices: a whole 4x4x8 slice. The times are simulated.
256 devices in a mesh: wide: 32 (over z, y), narrow: 8 (over x, core).
Axes of the slice: x: 4, y: 4, z: 8, core: 2. Of those that a mesh axis runs over, the one named last changes fastest.
Arguments:
- hidden: bfloat16 [65536, 8192], P('wide', 'narrow'), may hold values from -6 to 6
- base_key_value: bfloat16 [8192, 8, 2, 128], P('narrow'), may hold values from -0.0625 to 0.0625
- store_a: bfloat16 [256, 8192, 128], P('wide', 'narrow'), may hold values from -0.0625 to 0.0625
- stored_up_maps: bfloat16 [256, 2, 64, 8, 128], P('wide', None, None, 'narrow'), may hold values from -0.75 to 0.75
- adapter_ids: int32 [512], P('wide'), may hold values from 0 to 255, as said below
- span_start: int32 [512], P('wide'), may hold values from 0 to 31
Outputs:
- key_value: bfloat16 [8, 65536, 2, 128], P('narrow', 'wide')
Inputs may be any that keep to these rules, and one draw needn't show every extreme that they name: `adapter_ids`: requests of one replica that name different adapters name adapters of different owners, the owner of adapter a being the replica a // 8.
All inputs are finite; a program needn't handle non-finite values.
Results may differ from a plain program's by a relative error of at most 0.015.
Values may be sent and summed in bfloat16 or wider, within the bound.
No kernel may reach another device: no remote copies, remote signals or barrier semaphores. Data moves between devices by JAX's collectives and lax.ppermute only.
A program may use at most 192 MiB of HBM per device.

v0:
```python
import jax
import jax.numpy as jnp
from jax import lax
from jax.sharding import PartitionSpec as P

THETA = 500000.0


def rotate_keys(values, positions):
    half_dim = values.shape[-1] // 2
    frequency = THETA ** (-(jnp.arange(half_dim, dtype=jnp.float32) * 2.0 / values.shape[-1]))
    angles = positions[:, None] * frequency[None, :]
    angles = jnp.concatenate([angles, angles], axis=-1)
    turned = jnp.concatenate([-values[..., half_dim:], values[..., :half_dim]], axis=-1)
    return values * jnp.cos(angles) + turned * jnp.sin(angles)


def shards(hidden, base_key_value, store_a, stored_up_maps, adapter_ids, span_start):
    wide_count = lax.axis_size("wide")
    stored = store_a.shape[0]
    requests = adapter_ids.shape[0]
    span_len = hidden.shape[0] // requests
    rank_two = store_a.shape[2]
    owners = adapter_ids // stored
    slot_ids = adapter_ids % stored
    matches = owners[None, :] == jnp.arange(wide_count, dtype=jnp.int32)[:, None]
    wanted = jnp.max(jnp.where(matches, slot_ids[None, :] + 1, 0), axis=1).reshape(wide_count, 1)
    asked_slots = lax.all_to_all(wanted, "wide", split_axis=0, concat_axis=0, tiled=True)
    filled = asked_slots[:, 0] > 0
    chosen = jnp.maximum(asked_slots[:, 0] - 1, 0)
    reply_a = jnp.where(filled[:, None, None], store_a[chosen], jnp.zeros((), jnp.bfloat16))
    reply_b = jnp.where(
        filled[:, None, None, None, None], stored_up_maps[chosen], jnp.zeros((), jnp.bfloat16)
    )
    got_a, got_b = (
        lax.all_to_all(reply_a, "wide", split_axis=0, concat_axis=0, tiled=True),
        lax.all_to_all(reply_b, "wide", split_axis=0, concat_axis=0, tiled=True),
    )
    needed_a = got_a[owners]
    needed_b = got_b[owners]
    request_rows = hidden.reshape(requests, span_len, hidden.shape[1])
    shrink_part = jnp.einsum(
        "rtd,rdc->rtc", request_rows, needed_a, preferred_element_type=jnp.float32
    )
    shrunk = lax.psum(shrink_part.astype(jnp.bfloat16), "narrow")
    base_total_sum = lax.psum_scatter(
        jnp.einsum(
            "td,dhjc->htjc", hidden, base_key_value, preferred_element_type=jnp.float32
        ).astype(jnp.bfloat16),
        "narrow",
        scatter_dimension=0,
        tiled=True,
    ).astype(jnp.float32)
    rank = rank_two // 2
    shrunk_split = shrunk.reshape(requests, span_len, 2, rank)
    delta = jnp.einsum(
        "rtjk,rjkhc->hrtjc", shrunk_split, needed_b, preferred_element_type=jnp.float32
    )
    raw = base_total_sum + delta.reshape(base_total_sum.shape)
    positions = (
        (span_start[:, None] * span_len + jnp.arange(span_len, dtype=jnp.int32)[None, :])
        .reshape(-1)
        .astype(jnp.float32)
    )
    keys_turned = jax.vmap(lambda head_keys: rotate_keys(head_keys, positions))(raw[:, :, 0, :])
    joined = jnp.stack([keys_turned, raw[:, :, 1, :]], axis=2)
    return joined.astype(jnp.bfloat16)


def solution(mesh):
    placed = (
        P("wide", "narrow"),
        P("narrow", None, None, None),
        P("wide", "narrow", None),
        P("wide", None, None, "narrow", None),
        P("wide"),
        P("wide"),
    )
    return jax.shard_map(
        shards,
        mesh=mesh,
        in_specs=placed,
        out_specs=P("narrow", "wide", None, None),
        check_vma=False,
    )
```

profile of v0, /device:TPU:1, one launch (start us, length us, event | category | flops | bytes accessed | tf_op | source)
XLA Modules:
  0.0 383.8 jit_solution(11532929862729622991)
XLA Ops:
  6.5 0.8 compare_select_fusion
  7.4 0.1 select_reduce_fusion
  7.4 0.1 copy.22
  7.5 20.4 %all_to_all.19 = s32[32,1,1]{2,1,0:T(1,128)S(1)} all-to-all(s32[32,1,1]{2,1,0:T(1,128)S(1)} %copy.22), channel_id=1, replica_groups=mesh['wide'=32,'narrow'=8] {'wide'}, dimensions={0} | all-to-all | bytes 256 | tf_op jit(solution)/shard_map/all_to_all | solution.py:28
  28.0 0.7 maximum_reduce_fusion
  28.6 4.9 %gather_fusion.2 = bf16[32,1024,128]{2,1,0:T(8,128)(2,1)} fusion(bf16[8,1024,128]{2,1,0:T(8,128)(2,1)S(1)} %copy-done, s32[1024]{0:T(1024)S(1)} %pad_clamp_fusion.1), kind=kCustom, calls=%fused_computation.2 | custom fusion | bytes 16777344 | tf_op jit(solution)/shard_map/gather | solution.py:31
  33.5 0.7 compare_reduce_fusion
  34.2 7.2 %broadcast_select_fusion = bf16[32,1024,128]{2,1,0:T(8,128)(2,1)} fusion(bf16[32,1024,128]{2,1,0:T(8,128)(2,1)} %gather_fusion.2, pred[32]{0:T(512)(128)(4,1)S(1)} %compare_reduce_fusion), kind=kLoop, calls=%fused_computation.5 | loop fusion | flops 4194304 | bytes 16777248 | tf_op jit(solution)/shard_map/jit(_where)/select_n | solution.py:31
  41.4 5.0 %all-to-all-start.2 = ((bf16[32,1024,128]{2,1,0:T(8,128)(2,1)}), bf16[32,1024,128]{2,1,0:T(8,128)(2,1)}, u32[]{:S(2)}, u32[]{:S(2)}) async-start(bf16[32,1024,128]{2,1,0:T(8,128)(2,1)} %broadcast_select_fusion), calls=%async_computation.3 | async-start | bytes 16777216 | tf_op jit(solution)/shard_map/all_to_all | solution.py:36
  46.4 189.5 %all-to-all-done.2 = bf16[32,1024,128]{2,1,0:T(8,128)(2,1)} async-done(((bf16[32,1024,128]{2,1,0:T(8,128)(2,1)}), bf16[32,1024,128]{2,1,0:T(8,128)(2,1)}, u32[]{:S(2)}, u32[]{:S(2)}) %all-to-all-start.2) | async-done | bytes 8388640 | tf_op jit(solution)/shard_map/all_to_all | solution.py:36
  235.9 6.4 %gather_fusion.3 = bf16[16,1024,128]{2,1,0:T(8,128)(2,1)} fusion(bf16[32,1024,128]{2,1,0:T(8,128)(2,1)} %all-to-all-done.2, s32[1024]{0:T(1024)S(1)} %pad_clamp_fusion), kind=kCustom, calls=%fused_computation.3 | custom fusion | bytes 8388672 | tf_op jit(solution)/shard_map/gather | solution.py:39
  242.4 5.8 %convolution_convert_fusion = bf16[16,128,128]{2,1,0:T(8,128)(2,1)} fusion(bf16[16,1024,128]{2,1,0:T(8,128)(2,1)} %gather_fusion.3, bf16[16,128,1024]{2,1,0:T(8,128)(2,1)} %bitcast.39), kind=kOutput, calls=%fused_computation.10 | convolution fusion | flops 537133056 | bytes 8912896 | tf_op jit(solution)/shard_map/rtd,rdc->rtc/dot_general | solution.py:42
  248.2 14.5 %convert_bitcast_fusion = bf16[8,2048,2,128]{1,3,2,0:T(8,128)(2,1)} fusion(bf16[2048,1024]{1,0:T(8,128)(2,1)} %param.6, bf16[1024,8,2,128]{3,2,1,0:T(2,128)(2,1)} %param.7), kind=kOutput, calls=%fused_computation.4 | convolution fusion | flops 8594128896 | bytes 16777216 | tf_op jit(solution)/shard_map/td,dhjc->htjc/dot_general | solution.py:47
  262.7 0.9 copy-done.2
  263.6 0.7 gather_fusion
  264.4 1.1 bitcast_select_fusion
  265.5 5.8 %all-to-all-start.1 = ((bf16[32,2,64,1,128]{4,2,1,3,0:T(8,128)(2,1)}), bf16[32,2,64,1,128]{4,2,1,3,0:T(8,128)(2,1)S(1)}, u32[]{:S(2)}, u32[]{:S(2)}) async-start(bf16[32,2,64,1,128]{4,2,1,3,0:T(8,128)(2,1)} %bitcast_select_fusion), calls=%async_computation.2 | async-start | bytes 2097152 | tf_op jit(solution)/shard_map/all_to_all | solution.py:37
  271.3 0.1 convert_bitcast_fusion.1
  271.4 0.1 multiply_bitcast_fusion
  271.5 25.2 %all-to-all-done.1 = bf16[32,2,64,1,128]{4,2,1,3,0:T(8,128)(2,1)S(1)} async-done(((bf16[32,2,64,1,128]{4,2,1,3,0:T(8,128)(2,1)}), bf16[32,2,64,1,128]{4,2,1,3,0:T(8,128)(2,1)S(1)}, u32[]{:S(2)}, u32[]{:S(2)}) %all-to-all-start.1) | async-done | bytes 1048608 | tf_op jit(solution)/shard_map/all_to_all | solution.py:37
  296.7 0.6 gather_fusion.1
  297.3 13.9 %all-reduce.2.cloned.1.call-done = bf16[16,128,2,64]{1,3,2,0:T(8,128)(2,1)} async-done(((bf16[16,128,2,64]{1,3,2,0:T(8,128)(2,1)}), bf16[16,128,2,64]{1,3,2,0:T(8,128)(2,1)}) %all-reduce.2.cloned.1.call-update) | async-done | bytes 524304 | tf_op jit(solution)/shard_map/psum | solution.py:45
  311.2 1.5 convolution_bitcast_fusion
  312.7 2.0 copy.24
  314.7 1.7 reshape.278
  316.4 52.8 %reduce-scatter.2.cloned.1.call-done = bf16[1,2048,2,128]{1,3,2,0:T(8,128)(2,1)} async-done(((bf16[8,2048,2,128]{1,3,2,0:T(8,128)(2,1)}), bf16[1,2048,2,128]{1,3,2,0:T(8,128)(2,1)}) %reduce-scatter.2.cloned.1.call-update) | async-done | bytes 1048592 | tf_op jit(solution)/shard_map/reduce_scatter | solution.py:46
  369.2 1.5 convert_add_fusion
  370.7 0.1 slice_bitcast_fusion
  370.9 0.1 fusion.8
  371.0 3.9 %fusion.6 = bf16[1,2048,1,128]{1,3,2,0:T(8,128)(2,1)S(1)} fusion(f32[1,2048,1,64]{1,3,2,0:T(8,128)S(1)} %multiply_bitcast_fusion, f32[1,2048,1,64]{1,3,2,0:T(8,128)S(1)} %get-tuple-element.8, f32[1,2048,1,64]{1,3,2,0:T(8,128)S(1)} %get-tuple-element.7, f32[1,2048,2,128]{1,3,2,0:T(8,128)S(1)} %convert_add_fusion), kind=kLoop, calls=%fused_computation.17 | loop fusion | flops 1572864 | bytes 3145728 | tf_op jit(solution)/shard_map/convert
  374.8 0.1 pad_maximum_fusion.1
  374.9 2.0 copy.25
  (16 shorter events, 0.2 us)
Async XLA Ops:
  6.5 22.1 %copy-start = (bf16[8,1024,128]{2,1,0:T(8,128)(2,1)S(1)}, bf16[8,1024,128]{2,1,0:T(8,128)(2,1)}, u32[]{:S(2)}) copy-start(bf16[8,1024,128]{2,1,0:T(8,128)(2,1)} %param.8) | copy-start | bytes 6291460
  41.4 194.5 %all-to-all-start.2 = ((bf16[32,1024,128]{2,1,0:T(8,128)(2,1)}), bf16[32,1024,128]{2,1,0:T(8,128)(2,1)}, u32[]{:S(2)}, u32[]{:S(2)}) async-start(bf16[32,1024,128]{2,1,0:T(8,128)(2,1)} %broadcast_select_fusion), calls=%async_computation.3 | async-start | bytes 16777216 | tf_op jit(solution)/shard_map/all_to_all | solution.py:36
  46.3 264.8 %all-reduce.2.cloned.1.call-start = ((), (), s32[]{:S(2)}) async-start(), calls=%async_computation.5 | async-start | bytes 1048576 | tf_op jit(solution)/shard_map/psum | solution.py:45
  248.1 121.1 %reduce-scatter.2.cloned.1.call-start = ((), (), s32[]{:S(2)}) async-start(), calls=%async_computation.4 | async-start | bytes 9437184 | tf_op jit(solution)/shard_map/reduce_scatter | solution.py:46
  262.7 1.0 copy-start.2
  262.7 8.6 %copy-start.3 = (s32[16]{0:T(128)S(1)}, s32[16]{0:T(128)}, u32[]{:S(2)}) copy-start(s32[16]{0:T(128)} %param.11) | copy-start | bytes 196
  265.5 31.2 %all-to-all-start.1 = ((bf16[32,2,64,1,128]{4,2,1,3,0:T(8,128)(2,1)}), bf16[32,2,64,1,128]{4,2,1,3,0:T(8,128)(2,1)S(1)}, u32[]{:S(2)}, u32[]{:S(2)}) async-start(bf16[32,2,64,1,128]{4,2,1,3,0:T(8,128)(2,1)} %bitcast_select_fusion), calls=%async_computation.2 | async-start | bytes 2097152 | tf_op jit(solution)/shard_map/all_to_all | solution.py:37
  370.9 6.1 %copy-start.1 = (bf16[8,1024,128]{2,1,0:T(8,128)(2,1)S(1)}, bf16[8,1024,128]{2,1,0:T(8,128)(2,1)}, u32[]{:S(2)}) copy-start(bf16[8,1024,128]{2,1,0:T(8,128)(2,1)} %param.8) | copy-start | bytes 6291460
Sparse Core Ops, SparseCore 0:
  248.3 62.8 all-reduce.1
  313.7 55.4 reduce-scatter.1
where the time goes:
time: 384 us
  waiting for transfers between devices  281 us (73%)
  matrix products  21.8 us (6%)
  blocking collectives  20.4 us (5%)
  local copies, waits for them, and re-layouts  19.5 us (5%)
  other arithmetic  16.3 us (4%)
  between operations  13.6 us (4%)
  starting transfers between devices  10.8 us (3%)
    all_to_all x1, waiting for transfers between devices, shards(): lax.all_to_all(reply_a, 'wide', split_axis=0, concat_axis=0, tiled=True)  190 us
    reduce_scatter x1, waiting for transfers between devices, shards(): lax.psum_scatter(jnp.einsum('td,dhjc->htjc', hidden, base_key_value, pref...  52.8 us
    all_to_all x1, waiting for transfers between devices, shards(): lax.all_to_all(reply_b, 'wide', split_axis=0, concat_axis=0, tiled=True)  25.2 us
    all_to_all x1, blocking collectives, shards(): lax.all_to_all(wanted, 'wide', split_axis=0, concat_axis=0, tiled=True)  20.4 us
    dot_general x1, matrix products, shards(): jnp.einsum('td,dhjc->htjc', hidden, base_key_value, preferred_element_typ...  14.5 us
    psum x1, waiting for transfers between devices, shards(): shrunk = lax.psum(shrink_part.astype(jnp.bfloat16), 'narrow')  13.9 us
  transfers between devices with their start and end apart: 4, of which 4 were waited for; matrix products, arithmetic and copies ran while one was open for 6% of the time, Pallas kernels for 0%

commit v1 on v0

--- a/solution.py
+++ b/solution.py
@@ -42,7 +42,8 @@
     shrink_part = jnp.einsum(
         "rtd,rdc->rtc", request_rows, needed_a, preferred_element_type=jnp.float32
     )
-    shrunk = lax.psum(shrink_part.astype(jnp.bfloat16), "narrow")
+    load = shrink_part.astype(jnp.bfloat16)
+    shrunk = lax.all_gather(load, "narrow").sum(axis=0)
     base_total_sum = lax.psum_scatter(
         jnp.einsum(
             "td,dhjc->htjc", hidden, base_key_value, preferred_element_type=jnp.float32

time: 384 us -> 354 us (0.922)
  waiting for transfers between devices: 281 us -> 246 us
    reduce_scatter x1, waiting for transfers between devices: 52.8 us -> 31.6 us  [shards(): lax.psum_scatter(jnp.einsum('td,dhjc->htjc', hidden, base_key_value, pref...]
    psum x1 -> x0, waiting for transfers between devices: 13.9 us -> none  [shards(): shrunk = lax.psum(shrink_part.astype(jnp.bfloat16), 'narrow')]
  transfers between devices with their start and end apart: 4 -> 4, of which waited for: 4 -> 3; matrix products, arithmetic and copies ran while one was open for 6% -> 7% of each run, Pallas kernels for 0% -> 0%
where the time goes in v1:
time: 354 us; the launch traced here: 353 us
  waiting for transfers between devices  246 us (69%)
  local copies, waits for them, and re-layouts  21.6 us (6%)
  matrix products  21 us (6%)
  blocking collectives  20.4 us (6%)
  other arithmetic  19.3 us (5%)
  between operations  13.6 us (4%)
  starting transfers between devices  10.8 us (3%)
    all_to_all x1, waiting for transfers between devices, shards(): lax.all_to_all(reply_a, 'wide', split_axis=0, concat_axis=0, tiled=True)  190 us
    reduce_scatter x1, waiting for transfers between devices, shards(): lax.psum_scatter(jnp.einsum('td,dhjc->htjc', hidden, base_key_value, pref...  31.6 us
    all_to_all x1, waiting for transfers between devices, shards(): lax.all_to_all(reply_b, 'wide', split_axis=0, concat_axis=0, tiled=True)  25.2 us
    all_to_all x1, blocking collectives, shards(): lax.all_to_all(wanted, 'wide', split_axis=0, concat_axis=0, tiled=True)  20.4 us
    dot_general x1, matrix products, shards(): jnp.einsum('td,dhjc->htjc', hidden, base_key_value, preferred_element_typ...  14.5 us
    select_n x1, other arithmetic, shards(): jnp.where(filled[:, None, None], store_a[chosen], jnp.zeros((), jnp.bfloa...  7.22 us
  transfers between devices with their start and end apart: 4, of which 3 were waited for; matrix products, arithmetic and copies ran while one was open for 7% of the time, Pallas kernels for 0%

profile of v1, /device:TPU:1, one launch (start us, length us, event | category | flops | bytes accessed | tf_op | source)
XLA Modules:
  0.0 353.0 jit_solution(9496316345119658377)
XLA Ops:
  6.5 0.8 compare_select_fusion
  7.4 0.1 select_reduce_fusion
  7.4 0.1 copy.38
  7.5 20.4 %all_to_all.19 = s32[32,1,1]{2,1,0:T(1,128)S(1)} all-to-all(s32[32,1,1]{2,1,0:T(1,128)S(1)} %copy.38), channel_id=1, replica_groups=mesh['wide'=32,'narrow'=8] {'wide'}, dimensions={0} | all-to-all | bytes 256 | tf_op jit(solution)/shard_map/all_to_all | solution.py:28
  28.0 0.7 maximum_reduce_fusion
  28.6 4.9 %gather_fusion.2 = bf16[32,1024,128]{2,1,0:T(8,128)(2,1)} fusion(bf16[8,1024,128]{2,1,0:T(8,128)(2,1)S(1)} %copy-done, s32[1024]{0:T(1024)S(1)} %pad_clamp_fusion.1), kind=kCustom, calls=%fused_computation.2 | custom fusion | bytes 16777344 | tf_op jit(solution)/shard_map/gather | solution.py:31
  33.5 0.7 compare_reduce_fusion
  34.2 7.2 %broadcast_select_fusion = bf16[32,1024,128]{2,1,0:T(8,128)(2,1)} fusion(bf16[32,1024,128]{2,1,0:T(8,128)(2,1)} %gather_fusion.2, pred[32]{0:T(512)(128)(4,1)S(1)} %compare_reduce_fusion), kind=kLoop, calls=%fused_computation.5 | loop fusion | flops 4194304 | bytes 16777248 | tf_op jit(solution)/shard_map/jit(_where)/select_n | solution.py:31
  41.4 5.0 %all-to-all-start.2 = ((bf16[32,1024,128]{2,1,0:T(8,128)(2,1)}), bf16[32,1024,128]{2,1,0:T(8,128)(2,1)}, u32[]{:S(2)}, u32[]{:S(2)}) async-start(bf16[32,1024,128]{2,1,0:T(8,128)(2,1)} %broadcast_select_fusion), calls=%async_computation.3 | async-start | bytes 16777216 | tf_op jit(solution)/shard_map/all_to_all | solution.py:36
  46.4 189.5 %all-to-all-done.2 = bf16[32,1024,128]{2,1,0:T(8,128)(2,1)} async-done(((bf16[32,1024,128]{2,1,0:T(8,128)(2,1)}), bf16[32,1024,128]{2,1,0:T(8,128)(2,1)}, u32[]{:S(2)}, u32[]{:S(2)}) %all-to-all-start.2) | async-done | bytes 8388640 | tf_op jit(solution)/shard_map/all_to_all | solution.py:36
  235.9 6.4 %gather_fusion.3 = bf16[16,1024,128]{2,1,0:T(8,128)(2,1)} fusion(bf16[32,1024,128]{2,1,0:T(8,128)(2,1)} %all-to-all-done.2, s32[1024]{0:T(1024)S(1)} %pad_clamp_fusion), kind=kCustom, calls=%fused_computation.3 | custom fusion | bytes 8388672 | tf_op jit(solution)/shard_map/gather | solution.py:39
  242.4 4.9 %fusion.2 = bf16[16,128,128]{1,2,0:T(8,128)(2,1)S(1)} fusion(bf16[16,1024,128]{2,1,0:T(8,128)(2,1)} %gather_fusion.3, bf16[16,128,1024]{2,1,0:T(8,128)(2,1)} %bitcast.41), kind=kOutput, calls=%fused_computation.11 | convolution fusion | flops 537133056 | bytes 8912896 | tf_op jit(solution)/shard_map/rtd,rdc->rtc/dot_general | solution.py:42
  247.3 1.0 copy.40
  248.4 14.5 %convert_bitcast_fusion = bf16[8,2048,2,128]{1,3,2,0:T(8,128)(2,1)} fusion(bf16[2048,1024]{1,0:T(8,128)(2,1)} %param.6, bf16[1024,8,2,128]{3,2,1,0:T(2,128)(2,1)} %param.7), kind=kOutput, calls=%fused_computation.4 | convolution fusion | flops 8594128896 | bytes 16777216 | tf_op jit(solution)/shard_map/td,dhjc->htjc/dot_general | solution.py:48
  262.9 0.9 copy-done.2
  263.8 0.7 gather_fusion
  264.6 1.1 bitcast_select_fusion
  265.7 5.8 %all-to-all-start.1 = ((bf16[32,2,64,1,128]{4,2,1,3,0:T(8,128)(2,1)}), bf16[32,2,64,1,128]{4,2,1,3,0:T(8,128)(2,1)S(1)}, u32[]{:S(2)}, u32[]{:S(2)}) async-start(bf16[32,2,64,1,128]{4,2,1,3,0:T(8,128)(2,1)} %bitcast_select_fusion), calls=%async_computation.2 | async-start | bytes 2097152 | tf_op jit(solution)/shard_map/all_to_all | solution.py:37
  271.6 0.1 multiply_bitcast_fusion
  271.7 25.2 %all-to-all-done.1 = bf16[32,2,64,1,128]{4,2,1,3,0:T(8,128)(2,1)S(1)} async-done(((bf16[32,2,64,1,128]{4,2,1,3,0:T(8,128)(2,1)}), bf16[32,2,64,1,128]{4,2,1,3,0:T(8,128)(2,1)S(1)}, u32[]{:S(2)}, u32[]{:S(2)}) %all-to-all-start.1) | async-done | bytes 1048608 | tf_op jit(solution)/shard_map/all_to_all | solution.py:37
  296.9 1.4 gather_fusion.1
  298.3 3.0 reduce_sum.12
  301.2 0.3 copy.41
  301.5 1.5 convolution_bitcast_fusion
  303.1 2.0 copy.42
  305.0 1.8 reshape.278
  306.8 31.6 %reduce-scatter.2.cloned.1.call-done = bf16[1,2048,2,128]{1,3,2,0:T(8,128)(2,1)} async-done(((bf16[8,2048,2,128]{1,3,2,0:T(8,128)(2,1)}), bf16[1,2048,2,128]{1,3,2,0:T(8,128)(2,1)}) %reduce-scatter.2.cloned.1.call-update) | async-done | bytes 1048592 | tf_op jit(solution)/shard_map/reduce_scatter | solution.py:47
  338.4 1.5 convert_add_fusion
  340.1 0.1 fusion.9
  340.2 3.9 %fusion.7 = bf16[1,2048,1,128]{1,3,2,0:T(8,128)(2,1)S(1)} fusion(f32[1,2048,1,64]{1,3,2,0:T(8,128)S(1)} %multiply_bitcast_fusion, f32[1,2048,1,64]{1,3,2,0:T(8,128)S(1)} %get-tuple-element.8, f32[1,2048,1,64]{1,3,2,0:T(8,128)S(1)} %get-tuple-element.7, f32[1,2048,2,128]{1,3,2,0:T(8,128)S(1)} %convert_add_fusion), kind=kLoop, calls=%fused_computation.18 | loop fusion | flops 1572864 | bytes 3145728 | tf_op jit(solution)/shard_map/convert.1
  344.1 0.1 pad_maximum_fusion.1
  344.2 2.0 copy.43
  (19 shorter events, 0.4 us)
Async XLA Ops:
  6.5 22.1 %copy-start = (bf16[8,1024,128]{2,1,0:T(8,128)(2,1)S(1)}, bf16[8,1024,128]{2,1,0:T(8,128)(2,1)}, u32[]{:S(2)}) copy-start(bf16[8,1024,128]{2,1,0:T(8,128)(2,1)} %param.8) | copy-start | bytes 6291460
  41.4 194.5 %all-to-all-start.2 = ((bf16[32,1024,128]{2,1,0:T(8,128)(2,1)}), bf16[32,1024,128]{2,1,0:T(8,128)(2,1)}, u32[]{:S(2)}, u32[]{:S(2)}) async-start(bf16[32,1024,128]{2,1,0:T(8,128)(2,1)} %broadcast_select_fusion), calls=%async_computation.3 | async-start | bytes 16777216 | tf_op jit(solution)/shard_map/all_to_all | solution.py:36
  46.3 251.9 %all-gather.3.cloned.1.call-start = ((), (), s32[]{:S(2)}) async-start(), calls=%async_computation.5 | async-start | bytes 4718592 | tf_op jit(solution)/shard_map/all_gather | solution.py:46
  248.3 90.1 %reduce-scatter.2.cloned.1.call-start = ((), (), s32[]{:S(2)}) async-start(), calls=%async_computation.4 | async-start | bytes 9437184 | tf_op jit(solution)/shard_map/reduce_scatter | solution.py:47
  262.8 0.9 copy-start.2
  262.9 8.6 %copy-start.3 = (s32[16]{0:T(128)S(1)}, s32[16]{0:T(128)}, u32[]{:S(2)}) copy-start(s32[16]{0:T(128)} %param.11) | copy-start | bytes 196
  265.7 31.2 %all-to-all-start.1 = ((bf16[32,2,64,1,128]{4,2,1,3,0:T(8,128)(2,1)}), bf16[32,2,64,1,128]{4,2,1,3,0:T(8,128)(2,1)S(1)}, u32[]{:S(2)}, u32[]{:S(2)}) async-start(bf16[32,2,64,1,128]{4,2,1,3,0:T(8,128)(2,1)} %bitcast_select_fusion), calls=%async_computation.2 | async-start | bytes 2097152 | tf_op jit(solution)/shard_map/all_to_all | solution.py:37
  340.1 6.1 %copy-start.1 = (bf16[8,1024,128]{2,1,0:T(8,128)(2,1)S(1)}, bf16[8,1024,128]{2,1,0:T(8,128)(2,1)}, u32[]{:S(2)}) copy-start(bf16[8,1024,128]{2,1,0:T(8,128)(2,1)} %param.8) | copy-start | bytes 6291460
Sparse Core Ops, SparseCore 0:
  248.4 33.3 all-gather.2
  284.3 54.0 reduce-scatter.1
